TPU v7x, 32 devices: a whole 2x2x4 slice. The times are simulated.
32 devices in a mesh: section: 2 (over core), dp: 16 (over z, y, x).
Axes of the slice: x: 2, y: 2, z: 4, core: 2. Of those that a mesh axis runs over, the one named last changes fastest.
Arguments:
- acts: bfloat16 [2, 16, 1, 64, 2, 2, 128], P('section', 'dp'), may hold values from -6 to 6
- preacts: bfloat16 [2, 16, 1, 64, 2, 2, 128], P('section', 'dp'), may hold values from -6 to 6
- top_grad: bfloat16 [16, 1, 64, 2, 2, 128], P('dp'), may hold values from -6 to 6
- weights: bfloat16 [2, 64, 1728], P('section'), may hold values from -0.21875 to 0.21875
- a_factor: bfloat16 [2, 1728, 1728], P('section', 'dp'), as said below
- g_factor: bfloat16 [2, 64, 64], P('section'), as said below
Outputs:
- act_grads: bfloat16 [2, 16, 1, 64, 2, 2, 128], P('section', 'dp')
- update: float32 [2, 1728, 64], P('section', 'dp')
- inverse: float32 [2, 1728, 1728], P('section', 'dp')
Inputs may be any that keep to these rules, and one draw needn't show every extreme that they name: `a_factor`: each matrix is symmetric and positive definite. `g_factor`: each matrix is symmetric and positive definite.
All inputs are finite; a program needn't handle non-finite values. Where the computation divides by a largest or mean magnitude, that divisor is 1e-20 or more.
Results may differ from a plain program's by a relative error of at most 0.006.
Values may be sent and summed in bfloat16 or wider, within the bound.
No kernel may reach another device: no remote copies, remote signals or barrier semaphores. Data moves between devices by JAX's collectives and lax.ppermute only.
A program may use at most 64 MiB of HBM per device.

v0:
```python
import jax
import jax.numpy as jnp
from jax import lax
from jax.sharding import PartitionSpec as P

KW = 3
MICRO = 1


def shifted(value, axis, steps):
    count = lax.axis_size(axis)
    first, last = (max(0, -steps), min(count, count - steps))
    return lax.ppermute(value, axis, [(source, source + steps) for source in range(first, last)])


def tap_offsets(kernel_width):
    middle = kernel_width // 2
    result = []
    for along_x in range(kernel_width):
        for along_y in range(kernel_width):
            for along_z in range(kernel_width):
                result.append((along_x - middle, along_y - middle, along_z - middle))
    return result


def taps_stack(volume, kernel_width, direction):
    middle = kernel_width // 2
    padded = jnp.pad(volume, ((0, 0), (middle, middle), (middle, middle), (middle, middle)))
    size_x, size_y, size_z = (volume.shape[1], volume.shape[2], volume.shape[3])
    pieces = []
    for off_x, off_y, off_z in tap_offsets(kernel_width):
        start_x = middle + direction * off_x
        start_y = middle + direction * off_y
        start_z = middle + direction * off_z
        pieces.append(
            padded[
                :,
                start_x : start_x + size_x,
                start_y : start_y + size_y,
                start_z : start_z + size_z,
            ]
        )
    stacked = jnp.stack(pieces, 0)
    return stacked.reshape(len(pieces) * volume.shape[0], size_x * size_y * size_z)


def back_input(grad_out, w_rows):
    columns = taps_stack(grad_out, KW, -1)
    summed = lax.dot_general(
        w_rows, columns, (((0,), (0,)), ((), ())), preferred_element_type=jnp.float32
    )
    return summed.astype(jnp.bfloat16).reshape(grad_out.shape)


def back_weight(volume, grad_out):
    columns = taps_stack(volume, KW, 1)
    flattened = grad_out.reshape(grad_out.shape[0], -1)
    return lax.dot_general(
        columns, flattened, (((1,), (1,)), ((), ())), preferred_element_type=jnp.float32
    )


def local_inverse(matrix):
    values = matrix.astype(jnp.float32)
    step_size = 1.0 / jnp.max(jnp.sum(jnp.abs(values), axis=1))
    identity = jnp.eye(matrix.shape[0], dtype=jnp.float32)
    resid0 = (identity - step_size * values).astype(jnp.bfloat16)
    resid1 = jnp.dot(resid0, resid0, preferred_element_type=jnp.float32).astype(jnp.bfloat16)
    cross_term = jnp.dot(resid1, resid0, preferred_element_type=jnp.float32)
    return step_size * (
        identity + resid0.astype(jnp.float32) + resid1.astype(jnp.float32) + cross_term
    )


def eye_rows(start_row, row_total, order_full):
    column_ids = lax.broadcasted_iota(jnp.int32, (row_total, order_full), 1)
    row_ids = lax.broadcasted_iota(jnp.int32, (row_total, order_full), 0)
    return (column_ids == start_row + row_ids).astype(jnp.float32)


def doubling_sum(value, axis):
    count = lax.axis_size(axis)
    assert count & count - 1 == 0
    stride = 1
    while stride < count:
        value = value + lax.ppermute(value, axis, [(i, i ^ stride) for i in range(count)])
        stride *= 2
    return value


def shards(acts, preacts, top_grad, weights, a_factor, g_factor):
    section_index = lax.axis_index("section")
    section_count = lax.axis_size("section")
    tick_count = MICRO + section_count - 1
    gathered = lax.all_gather(a_factor[0], "dp", axis=0, tiled=True)
    inputs = acts[0, 0]
    pre_values = preacts[0, 0]
    upper_grads = top_grad[0]
    channels = weights.shape[1]
    w_rows = weights[0].reshape(channels, -1, channels).transpose(1, 0, 2).reshape(-1, channels)
    zero_field = jnp.zeros(inputs.shape[1:], jnp.bfloat16)

    def one_tick(tick_index, carried):
        outgoing, stored_grads, stored_slopes = carried
        incoming = shifted(outgoing, "section", -1)
        micro_index = tick_index - (section_count - 1 - section_index)
        is_valid = jnp.logical_and(micro_index >= 0, micro_index < MICRO)
        clipped = jnp.clip(micro_index, 0, MICRO - 1)
        from_top = lax.dynamic_index_in_dim(upper_grads, clipped, 0, keepdims=False)
        arriving = jnp.where(section_index == section_count - 1, from_top, incoming)
        pre_now = lax.dynamic_index_in_dim(pre_values, clipped, 0, keepdims=False)
        grad_out = jnp.where(pre_now > 0, arriving, zero_field)
        sending = back_input(grad_out, w_rows)
        old_grad = lax.dynamic_index_in_dim(stored_grads, clipped, 0, keepdims=False)
        old_slope = lax.dynamic_index_in_dim(stored_slopes, clipped, 0, keepdims=False)
        stored_grads = lax.dynamic_update_index_in_dim(
            stored_grads, jnp.where(is_valid, sending, old_grad), clipped, 0
        )
        stored_slopes = lax.dynamic_update_index_in_dim(
            stored_slopes, jnp.where(is_valid, grad_out, old_slope), clipped, 0
        )
        return (sending, stored_grads, stored_slopes)

    start_state = (
        zero_field,
        jnp.zeros(inputs.shape, jnp.bfloat16),
        jnp.zeros(inputs.shape, jnp.bfloat16),
    )
    last_sent, stored_grads, stored_slopes = lax.fori_loop(0, tick_count, one_tick, start_state)
    local_grad = back_weight(inputs[0], stored_slopes[0])
    summed_grad = doubling_sum(local_grad, "dp")
    mean_grad = summed_grad / lax.axis_size("dp")
    a_rows = a_factor[0]
    row_total = a_rows.shape[0]
    order_full = a_rows.shape[1]
    first_row = lax.axis_index("dp") * row_total
    full_values = gathered.astype(jnp.float32)
    step_size = 1.0 / jnp.max(jnp.sum(jnp.abs(full_values), axis=1))
    full_resid0 = (jnp.eye(order_full, dtype=jnp.float32) - step_size * full_values).astype(
        jnp.bfloat16
    )
    own_eye = eye_rows(first_row, row_total, order_full)
    resid0 = (own_eye - step_size * a_rows.astype(jnp.float32)).astype(jnp.bfloat16)
    resid1 = jnp.dot(resid0, full_resid0, preferred_element_type=jnp.float32).astype(jnp.bfloat16)
    cross_term = jnp.dot(resid1, full_resid0, preferred_element_type=jnp.float32)
    inverse_rows = step_size * (
        own_eye + resid0.astype(jnp.float32) + resid1.astype(jnp.float32) + cross_term
    )
    g_inverse = local_inverse(g_factor[0])
    preconditioned = jnp.dot(
        mean_grad, g_inverse, precision=lax.Precision.HIGHEST, preferred_element_type=jnp.float32
    )
    update_rows = jnp.dot(
        inverse_rows,
        preconditioned,
        precision=lax.Precision.HIGHEST,
        preferred_element_type=jnp.float32,
    )
    return (stored_grads[None, None], update_rows[None], inverse_rows[None])


def solution(mesh):
    placed = (
        P("section", "dp", None, None, None, None, None),
        P("section", "dp", None, None, None, None, None),
        P("dp", None, None, None, None, None),
        P("section", None, None),
        P("section", "dp", None),
        P("section", None, None),
    )
    return jax.shard_map(
        shards,
        mesh=mesh,
        in_specs=placed,
        out_specs=(
            P("section", "dp", None, None, None, None, None),
            P("section", "dp", None),
            P("section", "dp", None),
        ),
        check_vma=False,
    )
```

profile of v0, /device:TPU:7, one launch (start us, length us, event | category | flops | bytes accessed | tf_op | source)
XLA Modules:
  0.0 239.3 jit_solution(13392514546595699222)
XLA Ops:
  7.2 2.5 %copy.17 = bf16[1,108,1728]{2,0,1:T(2,128)(2,1)} copy(bf16[1,108,1728]{2,1,0:T(8,128)(2,1)} %param.12) | data formatting | bytes 746496 | tf_op args[4]
  9.8 0.5 reshape_squeeze.6
  10.3 0.9 copy.19
  12.6 0.2 fusion.89
  13.1 0.2 fusion.95
  13.4 0.2 fusion.99
  14.6 2.3 reshape.66
  16.9 0.7 broadcast.37
  17.5 0.6 broadcast.38
  18.2 24.4 %while.20 = (s32[]{:T(128)}, bf16[64,2,2,128]{3,2,1,0:T(2,128)(2,1)}, bf16[1,64,2,2,128]{4,3,2,1,0:T(2,128)(2,1)}, bf16[1,64,2,2,128]{4,3,2,1,0:T(2,128)(2,1)}, ...) while((s32[]{:T(128)}, ...), condition=%wide.region_1.2_spmd.clone, body=%wide.region_0.1_spmd.clone.sunk | while | flops 113475592 | bytes 10772739 | solution.py:129
  18.2 2.6 %collective-permute-start = (bf16[64,2,2,128]{3,2,1,0:T(2,128)(2,1)}, bf16[64,2,2,128]{3,2,1,0:T(2,128)(2,1)S(1)}, u32[]{:S(2)}, u32[]{:S(2)}) collective-permute-start(bf16[64,2,2,128]{3,2,1,0:T(2,128)(2,1)} %get-tuple-element.362), channel_id=1, source_target_pairs={{16,0},{17,1},{18,2},{19,3},{20,4},{21,5},{22,6},{23,7},{24,8},{25... | collective-permute-start | bytes 196616 | tf_op jit(solution)/shard_map/while/body/eval_jaxpr/ppermute | solution.py:13
  20.8 1.1 collective-permute-done
  21.9 1.7 fusion.172
  24.6 0.2 fusion.182
  24.9 0.2 fusion.184
  25.4 0.2 fusion.187
  26.9 0.7 reshape.81
  27.7 1.5 fusion.199
  29.2 0.6 reshape.82
  30.0 0.6 copy-done.3
  30.6 2.2 collective-permute-start
  32.8 1.1 collective-permute-done
  33.9 1.7 fusion.172
  37.5 0.2 fusion.187
  38.9 0.7 reshape.81
  39.7 1.5 fusion.199
  41.2 0.6 reshape.82
  42.0 0.6 copy-done.3
  42.6 0.9 reshape_squeeze.7
  43.5 2.1 fusion.130
  45.6 0.3 collective-permute-start.1
  45.9 21.8 %collective-permute-done.1 = f32[1728,64]{0,1:T(8,128)S(1)} collective-permute-done((f32[1728,64]{0,1:T(8,128)S(1)}, f32[1728,64]{0,1:T(8,128)S(1)}, u32[]{:S(2)}, u32[]{:S(2)}) %collective-permute-start.1) | collective-permute-done | bytes 442400 | tf_op jit(solution)/shard_map/ppermute | solution.py:86
  67.8 0.3 collective-permute-start.2
  68.1 10.9 %collective-permute-done.2 = f32[1728,64]{0,1:T(8,128)S(1)} collective-permute-done((f32[1728,64]{0,1:T(8,128)S(1)}, f32[1728,64]{0,1:T(8,128)S(1)}, u32[]{:S(2)}, u32[]{:S(2)}) %collective-permute-start.2) | collective-permute-done | bytes 442400 | tf_op jit(solution)/shard_map/ppermute | solution.py:86
  79.1 1.2 collective-permute-start.3
  80.3 0.6 reduce_max.19
  81.6 19.6 %collective-permute-done.3 = f32[1728,64]{0,1:T(8,128)S(1)} collective-permute-done((f32[1728,64]{0,1:T(8,128)S(1)}, f32[1728,64]{0,1:T(8,128)S(1)}, u32[]{:S(2)}, u32[]{:S(2)}) %collective-permute-start.3) | collective-permute-done | bytes 442400 | tf_op jit(solution)/shard_map/ppermute | solution.py:86
  101.3 2.3 collective-permute-start.4
  103.9 39.1 %collective-permute-done.4 = f32[1728,64]{0,1:T(8,128)S(1)} collective-permute-done((f32[1728,64]{0,1:T(8,128)S(1)}, f32[1728,64]{0,1:T(8,128)S(1)}, u32[]{:S(2)}, u32[]{:S(2)}) %collective-permute-start.4) | collective-permute-done | bytes 442400 | tf_op jit(solution)/shard_map/ppermute | solution.py:86
  142.9 0.6 fusion.61
  143.5 48.4 %all-gather.3.cloned.1.call-done = bf16[1,1728,1728]{2,0,1:T(2,128)(2,1)} async-done(((bf16[1,108,1728]{2,0,1:T(2,128)(2,1)}), bf16[1,1728,1728]{2,0,1:T(2,128)(2,1)}) %all-gather.3.cloned.1.call-update) | async-done | bytes 5971984 | tf_op jit(solution)/shard_map/all_gather | solution.py:95
  191.9 18.9 %abs_reduce_fusion = f32[1728]{0:T(1024)S(1)} fusion(bf16[1,1728,1728]{2,0,1:T(2,128)(2,1)} %all-gather.3.cloned.1.call-done), kind=kLoop, calls=%fused_computation.89 | loop fusion | flops 8956224 | bytes 5978880 | tf_op jit(solution)/shard_map/reduce_sum | solution.py:138
  210.8 0.6 reduce_max.18
  212.1 14.3 %convert_multiply_fusion = f32[1,1728,1728]{2,0,1:T(1,128)S(1)} fusion(bf16[1,1728,1728]{2,0,1:T(2,128)(2,1)} %all-gather.3.cloned.1.call-done, f32[]{:T(128)S(6)} %div.12), kind=kLoop, calls=%fused_computation.90 | loop fusion | flops 5971968 | bytes 17915908 | tf_op jit(solution)/shard_map/mul | solution.py:139
  226.5 1.3 convolution_convert_fusion.1
  227.8 1.4 fusion.55
  229.2 1.6 convolution_bitcast_fusion
  230.8 1.7 copy.18
  (102 shorter events, 9.6 us)
Async XLA Ops:
  7.2 2.7 %copy-start.4 = (bf16[1,64,1728]{2,1,0:T(8,128)(2,1)S(1)}, bf16[1,64,1728]{2,1,0:T(8,128)(2,1)}, u32[]{:S(2)}) copy-start(bf16[1,64,1728]{2,1,0:T(8,128)(2,1)} %param.11) | copy-start | bytes 663556
  7.2 4.1 %copy-start = (bf16[1,1,1,64,2,2,128]{6,5,4,3,2,1,0:T(2,128)(2,1)S(1)}, bf16[1,1,1,64,2,2,128]{6,5,4,3,2,1,0:T(2,128)(2,1)}, u32[]{:S(2)}) copy-start(bf16[1,1,1,64,2,2,128]{6,5,4,3,2,1,0:T(2,128)(2,1)} %param.8) | copy-start | bytes 196612
  7.2 184.7 %all-gather.3.cloned.1.call-start = ((), (), s32[]{:S(2)}) async-start(), calls=%async_computation | async-start | bytes 13160448 | tf_op jit(solution)/shard_map/all_gather | solution.py:95
  18.2 3.7 %collective-permute-start = (bf16[64,2,2,128]{3,2,1,0:T(2,128)(2,1)}, bf16[64,2,2,128]{3,2,1,0:T(2,128)(2,1)S(1)}, u32[]{:S(2)}, u32[]{:S(2)}) collective-permute-start(bf16[64,2,2,128]{3,2,1,0:T(2,128)(2,1)} %get-tuple-element.362), channel_id=1, source_target_pairs={{16,0},{17,1},{18,2},{19,3},{20,4},{21,5},{22,6},{23,7},{24,8},{25... | collective-permute-start | bytes 196616 | tf_op jit(solution)/shard_map/while/body/eval_jaxpr/ppermute | solution.py:13
  27.6 2.2 copy-start.2
  29.9 0.6 copy-start.3
  30.6 3.3 %collective-permute-start = (bf16[64,2,2,128]{3,2,1,0:T(2,128)(2,1)}, bf16[64,2,2,128]{3,2,1,0:T(2,128)(2,1)S(1)}, u32[]{:S(2)}, u32[]{:S(2)}) collective-permute-start(bf16[64,2,2,128]{3,2,1,0:T(2,128)(2,1)} %get-tuple-element.362), channel_id=1, source_target_pairs={{16,0},{17,1},{18,2},{19,3},{20,4},{21,5},{22,6},{23,7},{24,8},{25... | collective-permute-start | bytes 196616 | tf_op jit(solution)/shard_map/while/body/eval_jaxpr/ppermute | solution.py:13
  39.7 2.2 copy-start.2
  42.0 0.6 copy-start.3
  45.6 34.6 %copy-start.5 = (bf16[1,64,64]{2,1,0:T(8,128)(2,1)S(1)}, bf16[1,64,64]{2,1,0:T(8,128)(2,1)}, u32[]{:S(2)}) copy-start(bf16[1,64,64]{2,1,0:T(8,128)(2,1)} %param.13) | copy-start | bytes 24580
  45.6 22.1 %collective-permute-start.1 = (f32[1728,64]{0,1:T(8,128)S(1)}, f32[1728,64]{0,1:T(8,128)S(1)}, u32[]{:S(2)}, u32[]{:S(2)}) collective-permute-start(f32[1728,64]{0,1:T(8,128)S(1)} %fusion.130), channel_id=1, source_target_pairs={{0,1},{1,0},{2,3},{3,2},{4,5},{5,4},{6,7},{7,6},{8,9},{9,8},{10,11... | collective-permute-start | bytes 1327112 | tf_op jit(solution)/shard_map/ppermute | solution.py:86
  67.8 11.2 %collective-permute-start.2 = (f32[1728,64]{0,1:T(8,128)S(1)}, f32[1728,64]{0,1:T(8,128)S(1)}, u32[]{:S(2)}, u32[]{:S(2)}) collective-permute-start(f32[1728,64]{0,1:T(8,128)S(1)} %add.76), channel_id=1, source_target_pairs={{0,2},{1,3},{2,0},{3,1},{4,6},{5,7},{6,4},{7,5},{8,10},{9,11},{10,... | collective-permute-start | bytes 1327112 | tf_op jit(solution)/shard_map/ppermute | solution.py:86
  79.1 22.2 %collective-permute-start.3 = (f32[1728,64]{0,1:T(8,128)S(1)}, f32[1728,64]{0,1:T(8,128)S(1)}, u32[]{:S(2)}, u32[]{:S(2)}) collective-permute-start(f32[1728,64]{0,1:T(8,128)S(1)} %add.77), channel_id=1, source_target_pairs={{0,4},{1,5},{2,6},{3,7},{4,0},{5,1},{6,2},{7,3},{8,12},{9,13},{10,... | collective-permute-start | bytes 1327112 | tf_op jit(solution)/shard_map/ppermute | solution.py:86
  101.3 41.6 %collective-permute-start.4 = (f32[1728,64]{0,1:T(8,128)S(1)}, f32[1728,64]{0,1:T(8,128)S(1)}, u32[]{:S(2)}, u32[]{:S(2)}) collective-permute-start(f32[1728,64]{0,1:T(8,128)S(1)} %add.78), channel_id=1, source_target_pairs={{0,8},{1,9},{2,10},{3,11},{4,12},{5,13},{6,14},{7,15},{8,0},{9,1},... | collective-permute-start | bytes 1327112 | tf_op jit(solution)/shard_map/ppermute | solution.py:86
  212.1 14.3 %copy-start.1 = (bf16[1,108,1728]{2,1,0:T(8,128)(2,1)S(1)}, bf16[1,108,1728]{2,1,0:T(8,128)(2,1)}, u32[]{:S(2)}) copy-start(bf16[1,108,1728]{2,1,0:T(8,128)(2,1)} %param.12) | copy-start | bytes 1119748
Sparse Core Ops, SparseCore 0:
  11.4 180.4 all-gather.2
where the time goes:
time: 240 us; the launch traced here: 239 us
  waiting for transfers between devices  142 us (59%)
  other arithmetic  38.3 us (16%)
  local copies, waits for them, and re-layouts  24.1 us (10%)
  between operations  15.6 us (6%)
  matrix products  10.2 us (4%)
  starting transfers between devices  8.92 us (4%)
    ppermute x4, waiting for transfers between devices, doubling_sum(): lax.ppermute(value, axis, [(i, i ^ stride) for i in range(count)])  91.4 us
    all_gather x1, waiting for transfers between devices, shards(): gathered = lax.all_gather(a_factor[0], 'dp', axis=0, tiled=True)  48.4 us
    reduce_sum x1, other arithmetic, shards(): step_size = 1.0 / jnp.max(jnp.sum(jnp.abs(full_values), axis=1))  18.9 us
    mul x1, other arithmetic, shards(): step_size * full_values  14.3 us
    unnamed x37, local copies, waits for them, and re-layouts  8.38 us
    while x60, local copies, waits for them, and re-layouts  7.65 us
    ppermute x2, starting transfers between devices, shifted(): lax.ppermute(value, axis, [(source, source + steps) for source in range(f...  4.81 us
  transfers between devices with their start and end apart: 7, of which 7 were waited for; matrix products, arithmetic and copies ran while one was open for 12% of the time, Pallas kernels for 0%

commit v1 on v0

--- a/solution.py
+++ b/solution.py
@@ -92,7 +92,15 @@
     section_index = lax.axis_index("section")
     section_count = lax.axis_size("section")
     tick_count = MICRO + section_count - 1
-    gathered = lax.all_gather(a_factor[0], "dp", axis=0, tiled=True)
+    ways, here = (lax.axis_size("dp"), lax.axis_index("dp"))
+    grown, reach = (a_factor[0], 1)
+    while reach < ways:
+        theirs = lax.ppermute(grown, "dp", [(d, d ^ reach) for d in range(ways)])
+        mine_first = jnp.concatenate([grown, theirs], axis=0)
+        theirs_first = jnp.concatenate([theirs, grown], axis=0)
+        grown = jnp.where(here & reach == 0, mine_first, theirs_first)
+        reach = 2 * reach
+    gathered = grown
     inputs = acts[0, 0]
     pre_values = preacts[0, 0]
     upper_grads = top_grad[0]

time: 240 us -> 290 us (1.21)
  local copies, waits for them, and re-layouts: 24.1 us -> 75 us
  other arithmetic: 38.3 us -> 16.4 us
  waiting for transfers between devices: 142 us -> 162 us
  between operations: 15.6 us -> 2.2 us
  matrix products: 10.2 us -> 20.2 us
  starting transfers between devices: 8.92 us -> 12.9 us
    ppermute x4, waiting for transfers between devices: 91.4 us -> 141 us  [doubling_sum(): lax.ppermute(value, axis, [(i, i ^ stride) for i in range(count)])]
    all_gather x1 -> x0, waiting for transfers between devices: 48.4 us -> none  [shards(): gathered = lax.all_gather(a_factor[0], 'dp', axis=0, tiled=True)]
    while x60 -> x52, local copies, waits for them, and re-layouts: 7.65 us -> 37.6 us
    ppermute x0 -> x4, waiting for transfers between devices: none -> 19.2 us  [shards(): theirs = lax.ppermute(grown, 'dp', [(d, d ^ reach) for d in range(ways)])]
    mul x1 -> x0, other arithmetic: 14.3 us -> none  [shards(): step_size * full_values]
    unnamed x37 -> x40, local copies, waits for them, and re-layouts: 8.38 us -> 20.8 us
    reduce_sum x1, other arithmetic: 18.9 us -> 7.51 us  [shards(): step_size = 1.0 / jnp.max(jnp.sum(jnp.abs(full_values), axis=1))]
    reshape x3, local copies, waits for them, and re-layouts: 3.71 us -> 12.8 us  [taps_stack(): stacked.reshape(len(pieces) * volume.shape[0], size_x * size_y * size_z)]
  transfers between devices with their start and end apart: 7 -> 10, of which waited for: 7 -> 8; matrix products, arithmetic and copies ran while one was open for 12% -> 27% of each run, Pallas kernels for 0% -> 0%
where the time goes in v1:
time: 290 us; the launch traced here: 289 us
  waiting for transfers between devices  162 us (56%)
  local copies, waits for them, and re-layouts  75 us (26%)
  matrix products  20.2 us (7%)
  other arithmetic  16.4 us (6%)
  starting transfers between devices  12.9 us (4%)
    ppermute x4, waiting for transfers between devices, doubling_sum(): lax.ppermute(value, axis, [(i, i ^ stride) for i in range(count)])  141 us
    while x52, local copies, waits for them, and re-layouts  37.6 us
    unnamed x40, local copies, waits for them, and re-layouts  20.8 us
    ppermute x4, waiting for transfers between devices, shards(): theirs = lax.ppermute(grown, 'dp', [(d, d ^ reach) for d in range(ways)])  19.2 us
    reshape x3, local copies, waits for them, and re-layouts, taps_stack(): stacked.reshape(len(pieces) * volume.shape[0], size_x * size_y * size_z)  12.8 us
    dot_general x1, matrix products, shards(): jnp.dot(resid0, full_resid0, preferred_element_type=jnp.float32)  8.14 us
    dot_general x1, matrix products, shards(): jnp.dot(resid1, full_resid0, preferred_element_type=jnp.float32)  7.77 us
    reduce_sum x1, other arithmetic, shards(): step_size = 1.0 / jnp.max(jnp.sum(jnp.abs(full_values), axis=1))  7.51 us
  transfers between devices with their start and end apart: 10, of which 8 were waited for; matrix products, arithmetic and copies ran while one was open for 27% of the time, Pallas kernels for 0%

profile of v1, /device:TPU:7, one launch (start us, length us, event | category | flops | bytes accessed | tf_op | source)
XLA Modules:
  0.0 288.7 jit_solution(12008571441866292264)
XLA Ops:
  1.0 1.4 reshape_squeeze.6
  4.0 7.1 %collective-permute-done.1 = bf16[108,1728]{1,0:T(8,128)(2,1)S(1)} collective-permute-done((bf16[108,1728]{1,0:T(8,128)(2,1)}, bf16[108,1728]{1,0:T(8,128)(2,1)S(1)}, u32[]{:S(2)}, u32[]{:S(2)}) %collective-permute-start.1) | collective-permute-done | bytes 373280 | tf_op jit(solution)/shard_map/ppermute | solution.py:98
  11.7 0.7 fusion.79
  16.7 12.1 %collective-permute-done.2 = bf16[216,1728]{1,0:T(8,128)(2,1)S(1)} collective-permute-done((bf16[216,1728]{1,0:T(8,128)(2,1)S(1)}, bf16[216,1728]{1,0:T(8,128)(2,1)S(1)}, u32[]{:S(2)}, u32[]{:S(2)}) %collective-permute-start.2) | collective-permute-done | bytes 746528 | tf_op jit(solution)/shard_map/ppermute | solution.py:98
  28.7 1.6 maximum_select_fusion.2
  30.4 1.3 collective-permute-start.3
  31.8 58.1 %while.20 = (s32[]{:T(128)}, bf16[64,2,2,128]{3,2,1,0:T(2,128)(2,1)S(1)}, bf16[1,64,2,2,128]{4,3,2,1,0:T(2,128)(2,1)S(1)}, bf16[1,64,2,2,128]{4,3,2,1,0:T(2,128)...) while((s32[]{:T(128)}, ...), condition=%wide.region_1.2_spmd.clone, body=%wide.region_0.1_spmd.clone.sunk | while | flops 113475592 | bytes 10248395 | solution.py:137
  32.0 4.6 %collective-permute-start = (bf16[64,2,2,128]{3,2,1,0:T(2,128)(2,1)S(1)}, bf16[64,2,2,128]{3,2,1,0:T(2,128)(2,1)S(1)}, u32[]{:S(2)}, u32[]{:S(2)}) collective-permute-start(bf16[64,2,2,128]{3,2,1,0:T(2,128)(2,1)S(1)} %get-tuple-element.350), channel_id=1, source_target_pairs={{16,0},{17,1},{18,2},{19,3},{20,4},{21,5},{22,6},{23,7},{24,8},{25... | collective-permute-start | bytes 196616 | tf_op jit(solution)/shard_map/while/body/eval_jaxpr/ppermute | solution.py:13
  36.6 0.9 collective-permute-done
  43.3 0.7 fusion.191
  44.0 0.8 fusion.192
  45.5 0.8 fusion.194
  46.3 0.8 fusion.195
  47.7 0.8 fusion.196
  48.5 0.8 fusion.197
  50.0 0.8 fusion.199
  57.2 4.3 %reshape.73 = bf16[1728,512]{1,0:T(8,128)(2,1)S(1)} reshape(bf16[27,64,2,2,128]{4,3,2,1,0:T(2,128)(2,1)} %fusion.208) | data formatting | bytes 3538944 | tf_op jit(solution)/shard_map/while/body/eval_jaxpr/reshape | solution.py:44
  62.1 2.3 collective-permute-start
  64.4 0.9 collective-permute-done
  71.1 0.7 fusion.191
  71.8 0.8 fusion.192
  73.3 0.8 fusion.194
  74.1 0.8 fusion.195
  75.5 0.8 fusion.196
  76.3 0.8 fusion.197
  77.8 0.8 fusion.199
  85.0 4.3 %reshape.73 = bf16[1728,512]{1,0:T(8,128)(2,1)S(1)} reshape(bf16[27,64,2,2,128]{4,3,2,1,0:T(2,128)(2,1)} %fusion.208) | data formatting | bytes 3538944 | tf_op jit(solution)/shard_map/while/body/eval_jaxpr/reshape | solution.py:44
  89.9 0.8 fusion.93
  91.4 0.8 fusion.97
  92.2 0.8 fusion.99
  93.7 0.8 fusion.101
  94.4 0.8 fusion.103
  95.9 0.8 fusion.107
  96.7 0.7 fusion.109
  98.9 4.6 %maximum_select_fusion.1 = bf16[864,1728]{1,0:T(8,128)(2,1)} fusion(bf16[432,1728]{1,0:T(8,128)(2,1)} %collective-permute-done.3, bf16[432,1728]{1,0:T(8,128)(2,1)} %maximum_select_fusion.2, pred[]{:T(512)S(6)} %eq.44), kind=kLoop, calls=%fused_computation.122 | loop fusion | flops 13436928 | bytes 5971969 | tf_op jit(solution)/shard_map/jit(_where)/select_n | solution.py:101
  103.5 2.3 collective-permute-start.4
  109.3 0.7 fusion.125
  110.1 4.3 %reshape.66 = bf16[1728,512]{1,0:T(8,128)(2,1)S(1)} reshape(bf16[27,64,2,2,128]{4,3,2,1,0:T(2,128)(2,1)} %fusion.125) | data formatting | bytes 3538944 | tf_op jit(solution)/shard_map/reshape | solution.py:44
  115.4 11.3 %collective-permute-done.5 = f32[1728,64]{0,1:T(8,128)S(1)} collective-permute-done((f32[1728,64]{0,1:T(8,128)S(1)}, f32[1728,64]{0,1:T(8,128)S(1)}, u32[]{:S(2)}, u32[]{:S(2)}) %collective-permute-start.5) | collective-permute-done | bytes 442400 | tf_op jit(solution)/shard_map/ppermute | solution.py:86
  127.0 10.6 %collective-permute-done.6 = f32[1728,64]{0,1:T(8,128)S(1)} collective-permute-done((f32[1728,64]{0,1:T(8,128)S(1)}, f32[1728,64]{0,1:T(8,128)S(1)}, u32[]{:S(2)}, u32[]{:S(2)}) %collective-permute-start.6) | collective-permute-done | bytes 442400 | tf_op jit(solution)/shard_map/ppermute | solution.py:86
  139.3 42.7 %collective-permute-done.7 = f32[1728,64]{0,1:T(8,128)S(1)} collective-permute-done((f32[1728,64]{0,1:T(8,128)S(1)}, f32[1728,64]{0,1:T(8,128)S(1)}, u32[]{:S(2)}, u32[]{:S(2)}) %collective-permute-start.7) | collective-permute-done | bytes 442400 | tf_op jit(solution)/shard_map/ppermute | solution.py:86
  182.0 1.0 collective-permute-start.8
  183.3 76.2 %collective-permute-done.8 = f32[1728,64]{0,1:T(8,128)S(1)} collective-permute-done((f32[1728,64]{0,1:T(8,128)S(1)}, f32[1728,64]{0,1:T(8,128)S(1)}, u32[]{:S(2)}, u32[]{:S(2)}) %collective-permute-start.8) | collective-permute-done | bytes 442400 | tf_op jit(solution)/shard_map/ppermute | solution.py:86
  260.1 7.5 %fusion.54 = f32[1728]{0:T(1024)S(1)} fusion(bf16[864,1728]{1,0:T(8,128)(2,1)} %maximum_select_fusion.1, bf16[864,1728]{1,0:T(8,128)(2,1)} %collective-permute-done.4, pred[]{:T(512)S(6)} %eq.43), kind=kLoop, calls=%fused_computation.89 | loop fusion | flops 35830080 | bytes 5978881 | tf_op jit(solution)/shard_map/reduce_sum | solution.py:146
  268.9 8.1 %fusion.61 = bf16[108,1728]{1,0:T(8,128)(2,1)S(1)} fusion(f32[]{:T(128)S(6)} %div.12, s32[108]{0:T(128)S(1)} %iota_add_fusion, bf16[1,108,1728]{2,1,0:T(8,128)(2,1)S(1)} %copy-done.1, bf16[864,1728]{1,0:T(8,128)(2,1)} %collective-permute-done.4, bf16[864,1728]{1,0:T(8,128)(2,1)} %maximum_select_fusion.1, pred[]{:T(512)S(6)} %eq.43), kind=kOutput, calls=%fused_computation.123 | convolution fusion | flops 691068672 | bytes 6718901 | tf_op jit(solution)/shard_map/dot_general | solution.py:152
  277.0 7.8 %fusion.57 = f32[108,1728]{1,0:T(8,128)S(1)} fusion(bf16[108,1728]{1,0:T(8,128)(2,1)S(1)} %fusion.61, f32[]{:T(128)S(6)} %div.12, bf16[864,1728]{1,0:T(8,128)(2,1)} %collective-permute-done.4, bf16[864,1728]{1,0:T(8,128)(2,1)} %maximum_select_fusion.1, pred[]{:T(512)S(6)} %eq.43), kind=kOutput, calls=%fused_computation.94 | convolution fusion | flops 689762304 | bytes 7091717 | tf_op jit(solution)/shard_map/dot_general | solution.py:153
  285.2 1.9 convolution_bitcast_fusion
  287.0 1.7 copy.14
  (105 shorter events, 47.9 us)
Async XLA Ops:
  0.6 10.5 %copy-start.1 = (bf16[1,108,1728]{2,1,0:T(8,128)(2,1)S(1)}, bf16[1,108,1728]{2,1,0:T(8,128)(2,1)}, u32[]{:S(2)}) copy-start(bf16[1,108,1728]{2,1,0:T(8,128)(2,1)} %param.12) | copy-start | bytes 1119748
  0.6 1.9 copy-start
  0.6 10.5 %collective-permute-start.1 = (bf16[108,1728]{1,0:T(8,128)(2,1)}, bf16[108,1728]{1,0:T(8,128)(2,1)S(1)}, u32[]{:S(2)}, u32[]{:S(2)}) collective-permute-start(bf16[108,1728]{1,0:T(8,128)(2,1)} %bitcast.355), channel_id=1, source_target_pairs={{0,1},{1,0},{2,3},{3,2},{4,5},{5,4},{6,7},{7,6},{8,9},{9,8},{10,11... | collective-permute-start | bytes 1119752 | tf_op jit(solution)/shard_map/ppermute | solution.py:98
  11.4 17.4 %collective-permute-start.2 = (bf16[216,1728]{1,0:T(8,128)(2,1)S(1)}, bf16[216,1728]{1,0:T(8,128)(2,1)S(1)}, u32[]{:S(2)}, u32[]{:S(2)}) collective-permute-start(bf16[216,1728]{1,0:T(8,128)(2,1)S(1)} %maximum_select_fusion.3), channel_id=1, source_target_pairs={{0,2},{1,3},{2,0},{3,1},{4,6},{5,7},{6,4},{7,5},{8,10},{9,11},{10,... | collective-permute-start | bytes 2239496 | tf_op jit(solution)/shard_map/ppermute | solution.py:98
  15.3 16.5 %copy-start.3 = (bf16[1,1,1,64,2,2,128]{6,5,4,3,2,1,0:T(2,128)(2,1)S(1)}, bf16[1,1,1,64,2,2,128]{6,5,4,3,2,1,0:T(2,128)(2,1)}, u32[]{:S(2)}) copy-start(bf16[1,1,1,64,2,2,128]{6,5,4,3,2,1,0:T(2,128)(2,1)} %param.9) | copy-start | bytes 196612
  15.3 16.5 %copy-start.4 = (bf16[1,1,64,2,2,128]{5,4,3,2,1,0:T(2,128)(2,1)S(1)}, bf16[1,1,64,2,2,128]{5,4,3,2,1,0:T(2,128)(2,1)}, u32[]{:S(2)}) copy-start(bf16[1,1,64,2,2,128]{5,4,3,2,1,0:T(2,128)(2,1)} %param.10) | copy-start | bytes 196612
  30.4 68.5 %collective-permute-start.3 = (bf16[432,1728]{1,0:T(8,128)(2,1)}, bf16[432,1728]{1,0:T(8,128)(2,1)}, u32[]{:S(2)}, u32[]{:S(2)}) collective-permute-start(bf16[432,1728]{1,0:T(8,128)(2,1)} %maximum_select_fusion.2), channel_id=1, source_target_pairs={{0,4},{1,5},{2,6},{3,7},{4,0},{5,1},{6,2},{7,3},{8,12},{9,13},{10,... | collective-permute-start | bytes 4478984 | tf_op jit(solution)/shard_map/ppermute | solution.py:98
  32.0 5.5 %collective-permute-start = (bf16[64,2,2,128]{3,2,1,0:T(2,128)(2,1)S(1)}, bf16[64,2,2,128]{3,2,1,0:T(2,128)(2,1)S(1)}, u32[]{:S(2)}, u32[]{:S(2)}) collective-permute-start(bf16[64,2,2,128]{3,2,1,0:T(2,128)(2,1)S(1)} %get-tuple-element.350), channel_id=1, source_target_pairs={{16,0},{17,1},{18,2},{19,3},{20,4},{21,5},{22,6},{23,7},{24,8},{25... | collective-permute-start | bytes 196616 | tf_op jit(solution)/shard_map/while/body/eval_jaxpr/ppermute | solution.py:13
  62.1 3.1 %collective-permute-start = (bf16[64,2,2,128]{3,2,1,0:T(2,128)(2,1)S(1)}, bf16[64,2,2,128]{3,2,1,0:T(2,128)(2,1)S(1)}, u32[]{:S(2)}, u32[]{:S(2)}) collective-permute-start(bf16[64,2,2,128]{3,2,1,0:T(2,128)(2,1)S(1)} %get-tuple-element.350), channel_id=1, source_target_pairs={{16,0},{17,1},{18,2},{19,3},{20,4},{21,5},{22,6},{23,7},{24,8},{25... | collective-permute-start | bytes 196616 | tf_op jit(solution)/shard_map/while/body/eval_jaxpr/ppermute | solution.py:13
  89.9 13.6 %copy-start.2 = (bf16[1,64,2,2,128]{4,3,2,1,0:T(2,128)(2,1)}, bf16[1,64,2,2,128]{4,3,2,1,0:T(2,128)(2,1)S(1)}, u32[]{:S(2)}) copy-start(bf16[1,64,2,2,128]{4,3,2,1,0:T(2,128)(2,1)S(1)} %get-tuple-element.209) | copy-start | bytes 196612
  103.5 156.6 %collective-permute-start.4 = (bf16[864,1728]{1,0:T(8,128)(2,1)}, bf16[864,1728]{1,0:T(8,128)(2,1)}, u32[]{:S(2)}, u32[]{:S(2)}) collective-permute-start(bf16[864,1728]{1,0:T(8,128)(2,1)} %maximum_select_fusion.1), channel_id=1, source_target_pairs={{0,8},{1,9},{2,10},{3,11},{4,12},{5,13},{6,14},{7,15},{8,0},{9,1},... | collective-permute-start | bytes 8957960 | tf_op jit(solution)/shard_map/ppermute | solution.py:98
  115.0 22.8 %copy-start.5 = (bf16[1,64,64]{2,1,0:T(8,128)(2,1)S(1)}, bf16[1,64,64]{2,1,0:T(8,128)(2,1)}, u32[]{:S(2)}) copy-start(bf16[1,64,64]{2,1,0:T(8,128)(2,1)} %param.13) | copy-start | bytes 24580
  115.0 11.6 %collective-permute-start.5 = (f32[1728,64]{0,1:T(8,128)S(1)}, f32[1728,64]{0,1:T(8,128)S(1)}, u32[]{:S(2)}, u32[]{:S(2)}) collective-permute-start(f32[1728,64]{0,1:T(8,128)S(1)} %fusion.141), channel_id=1, source_target_pairs={{0,1},{1,0},{2,3},{3,2},{4,5},{5,4},{6,7},{7,6},{8,9},{9,8},{10,11... | collective-permute-start | bytes 1327112 | tf_op jit(solution)/shard_map/ppermute | solution.py:86
  126.7 10.9 %collective-permute-start.6 = (f32[1728,64]{0,1:T(8,128)S(1)}, f32[1728,64]{0,1:T(8,128)S(1)}, u32[]{:S(2)}, u32[]{:S(2)}) collective-permute-start(f32[1728,64]{0,1:T(8,128)S(1)} %add.76), channel_id=1, source_target_pairs={{0,2},{1,3},{2,0},{3,1},{4,6},{5,7},{6,4},{7,5},{8,10},{9,11},{10,... | collective-permute-start | bytes 1327112 | tf_op jit(solution)/shard_map/ppermute | solution.py:86
  137.6 44.3 %collective-permute-start.7 = (f32[1728,64]{0,1:T(8,128)S(1)}, f32[1728,64]{0,1:T(8,128)S(1)}, u32[]{:S(2)}, u32[]{:S(2)}) collective-permute-start(f32[1728,64]{0,1:T(8,128)S(1)} %add.77), channel_id=1, source_target_pairs={{0,4},{1,5},{2,6},{3,7},{4,0},{5,1},{6,2},{7,3},{8,12},{9,13},{10,... | collective-permute-start | bytes 1327112 | tf_op jit(solution)/shard_map/ppermute | solution.py:86
  182.0 77.5 %collective-permute-start.8 = (f32[1728,64]{0,1:T(8,128)S(1)}, f32[1728,64]{0,1:T(8,128)S(1)}, u32[]{:S(2)}, u32[]{:S(2)}) collective-permute-start(f32[1728,64]{0,1:T(8,128)S(1)} %add.78), channel_id=1, source_target_pairs={{0,8},{1,9},{2,10},{3,11},{4,12},{5,13},{6,14},{7,15},{8,0},{9,1},... | collective-permute-start | bytes 1327112 | tf_op jit(solution)/shard_map/ppermute | solution.py:86
